TPU v7x, 512 devices: a whole 4x4x16 slice. The times are simulated.
512 devices in a mesh: seq: 64 (over z, y), tp: 4 (over x), dp: 2 (over core).
Axes of the slice: x: 4, y: 4, z: 16, core: 2. Of those that a mesh axis runs over, the one named last changes fastest.
Arguments:
- inputs: bfloat16 [16384, 1280], P(('dp', 'seq'), 'tp'), parts along dimension 0, may hold values from -6 to 6
- out_grads: bfloat16 [16384, 1280], P(('dp', 'seq'), 'tp'), parts along dimension 0, may hold values from -6 to 6
- norm_gain: float32 [1280], replicated, may hold values from 0.1 to 1.9
- w_query: bfloat16 [640, 1280], P('tp'), may hold values from -0.15625 to 0.15625
- w_key: bfloat16 [640, 1280], P('tp'), may hold values from -0.15625 to 0.15625
- w_value: bfloat16 [640, 1280], P('tp'), may hold values from -0.15625 to 0.15625
- w_output: bfloat16 [640, 1280], P('tp'), may hold values from -0.25 to 0.25
- query_scale: float32 [80], replicated, may hold values from -4 to 4
- offsets: int32 [64], replicated, may hold values from 0 to 63, each once
Outputs:
- input_grads: bfloat16 [16384, 1280], P(('dp', 'seq'), 'tp'), parts along dimension 0
There are 2 independent parts, one for each index of `dp`. A program takes and returns all parts, laid end to end along the dimension named above; an argument that names none is the same for every part. Nothing has to cross between parts.
Inputs may be any that keep to these rules, and one draw needn't show every extreme that they name: `offsets`: each number appears exactly once.
All inputs are finite; a program needn't handle non-finite values.
Results may differ from a plain program's by a relative error of at most 0.007.
The roundings to bfloat16 on the way count: a program that leaves them out, or rounds other values in their place, can miss the bound.
Values may be sent and summed in bfloat16 or wider, within the bound.
No kernel may reach another device: no remote copies, remote signals or barrier semaphores. Data moves between devices by JAX's collectives and lax.ppermute only.
A program may use at most 64 MiB of HBM per device.

v0:
```python
import math
import jax
import jax.numpy as jnp
from jax import lax
from jax.sharding import PartitionSpec as P

PIECE = 128
scale_base = 1.4426950408889634
masked_score = -1e30
norm_eps = 1e-06


def positions_of(offsets, first_row, piece_rows, block_len):
    row_index = first_row + lax.iota(jnp.int32, piece_rows)
    shard_ids = row_index // block_len
    one_hot = (shard_ids[:, None] == lax.iota(jnp.int32, offsets.shape[0])[None, :]).astype(
        jnp.int32
    )
    return jnp.sum(one_hot * offsets[None, :], axis=1) * block_len + row_index % block_len


def column_scale(query_scale, head_count):
    head_width = query_scale.shape[0]
    factor = scale_base / math.sqrt(head_width) * jax.nn.softplus(query_scale)
    return jnp.tile(factor, head_count)


def split_heads(values, head_count):
    return values.reshape(values.shape[0], head_count, values.shape[1] // head_count)


def over_blocks(running, pieces, step_fn):
    piece_rows = pieces[0].shape[0]
    block_size = math.gcd(piece_rows, 512)

    def visit_block(number, state_now):
        first_row = number * block_size
        block_parts = tuple(
            (lax.dynamic_slice_in_dim(piece, first_row, block_size, 0) for piece in pieces)
        )
        return step_fn(state_now, block_parts, first_row)

    return lax.fori_loop(0, piece_rows // block_size, visit_block, running)


def per_device(
    inputs, out_grads, norm_gain, w_query, w_key, w_value, w_output, query_scale, offsets
):
    row_count = inputs.shape[0]
    width_here = inputs.shape[1]
    head_width = query_scale.shape[0]
    heads_here = w_query.shape[0] // head_width
    contract = (((1,), (1,)), ((), ()))
    full_inputs, full_grads = (
        lax.all_gather(inputs, "tp", axis=1, tiled=True),
        lax.all_gather(out_grads, "tp", axis=1, tiled=True),
    )
    full_width = full_inputs.shape[1]
    widened = full_inputs.astype(jnp.float32)
    inverse = lax.rsqrt(jnp.mean(widened * widened, axis=1, keepdims=True) + norm_eps)
    normed = (widened * inverse * norm_gain[None, :]).astype(jnp.bfloat16)
    factor = column_scale(query_scale, heads_here)
    queries = (
        lax.dot_general(normed, w_query, contract, preferred_element_type=jnp.float32)
        * factor[None, :]
    ).astype(jnp.bfloat16)
    key_rows = lax.dot_general(normed, w_key, contract, preferred_element_type=jnp.float32).astype(
        jnp.bfloat16
    )
    values = lax.dot_general(normed, w_value, contract, preferred_element_type=jnp.float32).astype(
        jnp.bfloat16
    )
    head_grads = lax.dot_general(
        full_grads, w_output, contract, preferred_element_type=jnp.float32
    ).astype(jnp.bfloat16)
    seq_index = lax.axis_index("seq")
    own_positions = positions_of(offsets, seq_index * row_count, row_count, PIECE)
    query_heads = split_heads(queries, heads_here)
    grad_heads = split_heads(head_grads, heads_here)
    key_heads = split_heads(key_rows, heads_here)
    value_heads = split_heads(values, heads_here)

    def peak_step(running, block_parts, first_row):
        key_part = block_parts[0]
        key_place = positions_of(offsets, first_row, key_part.shape[0], PIECE)
        row_peak, summed = running
        raw_scores = jnp.einsum(
            "qhd,khd->hqk",
            query_heads,
            split_heads(key_part, heads_here),
            preferred_element_type=jnp.float32,
        )
        visible = key_place[None, None, :] <= own_positions[None, :, None]
        masked = jnp.where(visible, raw_scores, masked_score)
        fresh_peak = jnp.maximum(row_peak, jnp.max(masked, axis=2))
        fresh_terms = jnp.where(visible, jnp.exp(masked - fresh_peak[:, :, None]), 0.0)
        summed = summed * jnp.exp(row_peak - fresh_peak) + jnp.sum(fresh_terms, axis=2)
        return (fresh_peak, summed)

    def make_grad_step(log_total):

        def grad_step(running, block_parts, first_row):
            key_part, value_part = block_parts
            key_place = positions_of(offsets, first_row, key_part.shape[0], PIECE)
            row_delta, first_sum, second_sum = running
            key_heads_part = split_heads(key_part, heads_here)
            raw_scores = jnp.einsum(
                "qhd,khd->hqk", query_heads, key_heads_part, preferred_element_type=jnp.float32
            )
            visible = key_place[None, None, :] <= own_positions[None, :, None]
            attend = jnp.exp(jnp.where(visible, raw_scores - log_total[:, :, None], masked_score))
            grad_probs = jnp.einsum(
                "qhd,khd->hqk",
                grad_heads,
                split_heads(value_part, heads_here),
                preferred_element_type=jnp.float32,
            )
            weighted = attend * grad_probs
            row_delta = row_delta + jnp.sum(weighted, axis=2)
            first_sum = first_sum + jnp.einsum(
                "hqk,khd->hqd",
                weighted.astype(jnp.bfloat16),
                key_heads_part,
                preferred_element_type=jnp.float32,
            )
            second_sum = second_sum + jnp.einsum(
                "hqk,khd->hqd",
                attend.astype(jnp.bfloat16),
                key_heads_part,
                preferred_element_type=jnp.float32,
            )
            return (row_delta, first_sum, second_sum)

        return grad_step

    peak_start = (
        jnp.full((heads_here, row_count), masked_score, jnp.float32),
        jnp.zeros((heads_here, row_count), jnp.float32),
    )
    grad_start = (
        jnp.zeros((heads_here, row_count), jnp.float32),
        jnp.zeros((heads_here, row_count, head_width), jnp.float32),
        jnp.zeros((heads_here, row_count, head_width), jnp.float32),
    )
    row_peak, summed = over_blocks(
        peak_start, (lax.all_gather(key_rows, "seq", axis=0, tiled=True),), peak_step
    )
    log_total = row_peak + jnp.log(summed)
    grad_step = make_grad_step(log_total)
    row_delta, first_sum, second_sum = over_blocks(
        grad_start,
        (
            lax.all_gather(key_rows, "seq", axis=0, tiled=True),
            lax.all_gather(values, "seq", axis=0, tiled=True),
        ),
        grad_step,
    )
    query_grad = first_sum - row_delta[:, :, None] * second_sum
    query_grad = jnp.transpose(query_grad, (1, 0, 2)).reshape(row_count, heads_here * head_width)
    query_done = (query_grad * factor[None, :]).astype(jnp.bfloat16)
    log_all, delta_all = (
        lax.all_gather(log_total.T, "seq", axis=0, tiled=True),
        lax.all_gather(row_delta.T, "seq", axis=0, tiled=True),
    )

    def key_step(running, block_parts, first_row):
        query_part, grad_part = block_parts
        piece_rows = query_part.shape[0]
        query_place = positions_of(offsets, first_row, piece_rows, PIECE)
        log_part = lax.dynamic_slice_in_dim(log_all, first_row, piece_rows, 0).T
        delta_part = lax.dynamic_slice_in_dim(delta_all, first_row, piece_rows, 0).T
        key_grad, value_grad = running
        query_heads_part = split_heads(query_part, heads_here)
        grad_heads_part = split_heads(grad_part, heads_here)
        raw_scores = jnp.einsum(
            "qhd,khd->hqk", query_heads_part, key_heads, preferred_element_type=jnp.float32
        )
        visible = own_positions[None, None, :] <= query_place[None, :, None]
        attend = jnp.exp(jnp.where(visible, raw_scores - log_part[:, :, None], masked_score))
        grad_probs = jnp.einsum(
            "qhd,khd->hqk", grad_heads_part, value_heads, preferred_element_type=jnp.float32
        )
        score_grad = (attend * (grad_probs - delta_part[:, :, None])).astype(jnp.bfloat16)
        key_grad = key_grad + jnp.einsum(
            "hqk,qhd->khd", score_grad, query_heads_part, preferred_element_type=jnp.float32
        )
        value_grad = value_grad + jnp.einsum(
            "hqk,qhd->khd",
            attend.astype(jnp.bfloat16),
            grad_heads_part,
            preferred_element_type=jnp.float32,
        )
        return (key_grad, value_grad)

    key_start = (
        jnp.zeros((row_count, heads_here, head_width), jnp.float32),
        jnp.zeros((row_count, heads_here, head_width), jnp.float32),
    )
    key_grad, value_grad = over_blocks(
        key_start,
        (
            lax.all_gather(queries, "seq", axis=0, tiled=True),
            lax.all_gather(head_grads, "seq", axis=0, tiled=True),
        ),
        key_step,
    )
    key_done = key_grad.reshape(row_count, heads_here * head_width).astype(jnp.bfloat16)
    value_done = value_grad.reshape(row_count, heads_here * head_width).astype(jnp.bfloat16)
    back_sum = jnp.dot(query_done, w_query, preferred_element_type=jnp.float32)
    back_sum = back_sum + jnp.dot(key_done, w_key, preferred_element_type=jnp.float32)
    back_sum = back_sum + jnp.dot(value_done, w_value, preferred_element_type=jnp.float32)
    start_col = lax.axis_index("tp") * width_here
    total_back = lax.psum(back_sum, "tp")
    scaled = total_back * norm_gain[None, :]
    row_dot = jnp.sum(widened * scaled, axis=1, keepdims=True)
    branch = inverse * scaled - widened * inverse * inverse * inverse * row_dot / full_width
    result = out_grads.astype(jnp.float32) + lax.dynamic_slice_in_dim(
        branch, start_col, width_here, 1
    )
    return result.astype(jnp.bfloat16)


def solution(mesh):
    return jax.shard_map(
        per_device,
        mesh=mesh,
        in_specs=(
            P(("dp", "seq"), "tp"),
            P(("dp", "seq"), "tp"),
            P(),
            P("tp", None),
            P("tp", None),
            P("tp", None),
            P("tp", None),
            P(),
            P(),
        ),
        out_specs=P(("dp", "seq"), "tp"),
        check_vma=False,
    )
```

profile of v0, /device:TPU:8, one launch (start us, length us, event | category | flops | bytes accessed | tf_op | source)
XLA Modules:
  0.0 678.4 jit_solution(6673104376951234624)
XLA Ops:
  6.6 13.1 %all_gather.25 = bf16[128,1280]{0,1:T(8,128)(2,1)S(1)} all-gather(bf16[128,320]{0,1:T(8,128)(2,1)} %param.15), channel_id=1, replica_groups=mesh['seq'=64,'tp'=4,'dp'=2] {'tp'}, dimensions={1}, use_global_device_ids=true | all-gather | bytes 409600 | tf_op jit(solution)/shard_map/all_gather | solution.py:55
  19.9 2.1 convolution_convert_fusion.2
  22.0 2.1 convolution_convert_fusion.1
  25.4 12.4 %all_gather.28 = bf16[128,1280]{0,1:T(8,128)(2,1)S(1)} all-gather(bf16[128,320]{0,1:T(8,128)(2,1)S(1)} %copy-done.6), channel_id=1, replica_groups=mesh['seq'=64,'tp'=4,'dp'=2] {'tp'}, dimensions={1}, use_global_device_ids=true | all-gather | bytes 409600 | tf_op jit(solution)/shard_map/all_gather | solution.py:56
  39.0 125.1 %all-gather.5.cloned.1.call-done = bf16[8192,160]{0,1:T(8,128)(2,1)} async-done(((bf16[128,160]{0,1:T(8,128)(2,1)}), bf16[8192,160]{0,1:T(8,128)(2,1)}) %all-gather.5.cloned.1.call-update) | async-done | bytes 2621456 | tf_op jit(solution)/shard_map/all_gather | solution.py:153
  164.1 39.6 %while.56 = (s32[]{:T(128)}, f32[2,128]{1,0:T(2,128)S(1)}, f32[2,128]{1,0:T(2,128)S(1)}, s32[64]{0:T(128)S(1)}, s32[128]{0:T(128)S(1)}, /*index=5*/bf16[8192,160...) while((s32[]{:T(128)}, f32[2,128]{1,0:T(2,128)S(1)}, ...), condition=%wide.region_6.7_spmd.clone, body=%wide.region_2.6_spmd.clone.sunk | while | flops 21806852 | bytes 1804210 | solution.py:43
  165.3 1.1 fusion.103
  167.8 1.1 fusion.103
  170.2 1.1 fusion.103
  172.7 1.1 fusion.103
  175.2 1.1 fusion.103
  177.7 1.1 fusion.103
  180.1 1.1 fusion.103
  182.6 1.1 fusion.103
  185.1 1.1 fusion.103
  187.6 1.1 fusion.103
  190.1 1.1 fusion.103
  192.5 1.1 fusion.103
  195.0 1.1 fusion.103
  197.5 1.1 fusion.103
  200.0 1.1 fusion.103
  202.4 1.1 fusion.103
  203.7 97.4 %all-gather.7.cloned.1.call-done = bf16[8192,160]{0,1:T(8,128)(2,1)} async-done(((bf16[128,160]{0,1:T(8,128)(2,1)}), bf16[8192,160]{0,1:T(8,128)(2,1)}) %all-gather.7.cloned.1.call-update) | async-done | bytes 2621456 | tf_op jit(solution)/shard_map/all_gather | solution.py:154
  301.1 50.2 %while.57 = (s32[]{:T(128)}, f32[2,128]{1,0:T(2,128)S(1)}, f32[2,128,80]{1,2,0:T(8,128)S(1)}, f32[2,128,80]{1,2,0:T(8,128)S(1)}, s32[64]{0:T(128)S(1)}, /*index=...) while((s32[]{:T(128)}, f32[2,128]{1,0:T(2,128)S(1)}, ...), condition=%wide.region_10.11_spmd.clone, body=%wide.region_7.10_spmd.clone.sunk | while | flops 84933376 | bytes 3966931 | solution.py:43
  302.4 1.1 fusion.115
  305.5 1.1 fusion.115
  308.7 1.1 fusion.115
  311.8 1.1 fusion.115
  314.9 1.1 fusion.115
  318.1 1.1 fusion.115
  321.2 1.1 fusion.115
  324.4 1.1 fusion.115
  327.5 1.1 fusion.115
  330.6 1.1 fusion.115
  333.8 1.1 fusion.115
  336.9 1.1 fusion.115
  340.1 1.1 fusion.115
  343.2 1.1 fusion.115
  346.3 1.1 fusion.115
  349.5 1.1 fusion.115
  351.3 80.1 %all_gather.32 = f32[8192,2]{0,1:T(2,128)S(1)} all-gather(f32[128,2]{0,1:T(2,128)S(1)} %bitcast.134), channel_id=1, replica_groups=mesh['seq'=64,'tp'=4,'dp'=2] {'seq'}, dimensions={0}, use_global_device_ids=true | all-gather | bytes 66560 | tf_op jit(solution)/shard_map/all_gather | solution.py:163
  431.4 80.0 %all_gather.30 = f32[8192,2]{0,1:T(2,128)S(1)} all-gather(f32[128,2]{0,1:T(2,128)S(1)} %bitcast.133), channel_id=1, replica_groups=mesh['seq'=64,'tp'=4,'dp'=2] {'seq'}, dimensions={0}, use_global_device_ids=true | all-gather | bytes 66560 | tf_op jit(solution)/shard_map/all_gather | solution.py:162
  511.4 63.3 %all-gather.11.cloned.1.call-done = bf16[8192,160]{0,1:T(8,128)(2,1)} async-done(((bf16[128,160]{0,1:T(8,128)(2,1)}), bf16[8192,160]{0,1:T(8,128)(2,1)}) %all-gather.11.cloned.1.call-update) | async-done | bytes 2621456 | tf_op jit(solution)/shard_map/all_gather | solution.py:203
  574.8 37.7 %while.58 = (s32[]{:T(128)}, f32[128,2,80]{0,2,1:T(8,128)S(1)}, f32[128,2,80]{0,2,1:T(8,128)S(1)}, bf16[8192,160]{0,1:T(8,128)(2,1)}, s32[128]{0:T(128)S(1)}, /*...) while((s32[]{:T(128)}, f32[128,2,80]{0,2,1:T(8,128)S(1)}, ...), condition=%wide.region_13.14_spmd.clone, body=%wide.region_11.13_spmd.clone.sunk | while | flops 84933120 | bytes 3462102 | solution.py:43
  574.8 1.1 constant_dynamic-slice_fusion.10
  613.5 1.2 convolution_add_fusion.2
  614.7 55.1 %all-reduce.2.cloned.1.call-done = f32[128,1280]{0,1:T(8,128)} async-done(((f32[128,1280]{0,1:T(8,128)}), f32[128,1280]{0,1:T(8,128)}) %all-reduce.2.cloned.1.call-update) | async-done | bytes 655376 | tf_op jit(solution)/shard_map/psum | solution.py:213
  669.8 1.3 fusion.33
  (489 shorter events, 93.2 us)
Async XLA Ops:
  6.5 17.7 %copy-start = (bf16[160,1280]{1,0:T(8,128)(2,1)S(1)}, bf16[160,1280]{1,0:T(8,128)(2,1)}, u32[]{:S(2)}) copy-start(bf16[160,1280]{1,0:T(8,128)(2,1)} %param.18) | copy-start | bytes 1228804
  6.5 17.7 %copy-start.9 = (f32[1280]{0:T(1024)S(1)}, f32[1280]{0:T(1024)}, u32[]{:S(2)}) copy-start(f32[1280]{0:T(1024)} %param.17) | copy-start | bytes 15364
  6.5 17.6 %copy-start.10 = (f32[80]{0:T(128)S(1)}, f32[80]{0:T(128)}, u32[]{:S(2)}) copy-start(f32[80]{0:T(128)} %param.22) | copy-start | bytes 964
  6.5 18.9 %copy-start.6 = (bf16[128,320]{0,1:T(8,128)(2,1)S(1)}, bf16[128,320]{0,1:T(8,128)(2,1)}, u32[]{:S(2)}) copy-start(bf16[128,320]{0,1:T(8,128)(2,1)} %param.16) | copy-start | bytes 245764
  6.5 31.3 %copy-start.5 = (bf16[160,1280]{1,0:T(8,128)(2,1)S(1)}, bf16[160,1280]{1,0:T(8,128)(2,1)}, u32[]{:S(2)}) copy-start(bf16[160,1280]{1,0:T(8,128)(2,1)} %param.21) | copy-start | bytes 1228804
  6.5 32.3 %copy-start.7 = (s32[64]{0:T(128)S(1)}, s32[64]{0:T(128)}, u32[]{:S(2)}) copy-start(s32[64]{0:T(128)} %param.23) | copy-start | bytes 772
  6.6 157.5 %all-gather.5.cloned.1.call-start = ((), (), s32[]{:S(2)}) async-start(), calls=%async_computation | async-start | bytes 2662400 | tf_op jit(solution)/shard_map/all_gather | solution.py:153
  22.0 279.1 %all-gather.7.cloned.1.call-start = ((), (), s32[]{:S(2)}) async-start(), calls=%async_computation.1 | async-start | bytes 2662400 | tf_op jit(solution)/shard_map/all_gather | solution.py:154
  24.1 487.3 %all-gather.9.cloned.1.call-start = ((), (), s32[]{:S(2)}) async-start(), calls=%async_computation.2 | async-start | bytes 2662400 | tf_op jit(solution)/shard_map/all_gather | solution.py:202
  25.4 549.4 %all-gather.11.cloned.1.call-start = ((), (), s32[]{:S(2)}) async-start(), calls=%async_computation.3 | async-start | bytes 2662400 | tf_op jit(solution)/shard_map/all_gather | solution.py:203
  38.7 631.1 %all-reduce.2.cloned.1.call-start = ((), (), s32[]{:S(2)}) async-start(), calls=%async_computation.4 | async-start | bytes 1310720 | tf_op jit(solution)/shard_map/psum | solution.py:213
  164.1 137.0 %copy-start.1 = (bf16[128,160]{0,1:T(8,128)(2,1)S(1)}, bf16[128,160]{0,1:T(8,128)(2,1)}, u32[]{:S(2)}) copy-start(bf16[128,160]{0,1:T(8,128)(2,1)} %convolution_convert_fusion) | copy-start | bytes 122884
  301.1 273.7 %copy-start.2 = (bf16[128,160]{0,1:T(8,128)(2,1)S(1)}, bf16[128,160]{0,1:T(8,128)(2,1)}, u32[]{:S(2)}) copy-start(bf16[128,160]{0,1:T(8,128)(2,1)} %convolution_convert_fusion.1) | copy-start | bytes 122884
  301.1 273.7 %copy-start.8 = (bf16[128,160]{0,1:T(8,128)(2,1)S(1)}, bf16[128,160]{0,1:T(8,128)(2,1)}, u32[]{:S(2)}) copy-start(bf16[128,160]{0,1:T(8,128)(2,1)} %convolution_convert_fusion.2) | copy-start | bytes 122884
  574.8 38.2 %copy-start.3 = (bf16[160,1280]{1,0:T(8,128)(2,1)S(1)}, bf16[160,1280]{1,0:T(8,128)(2,1)}, u32[]{:S(2)}) copy-start(bf16[160,1280]{1,0:T(8,128)(2,1)} %param.19) | copy-start | bytes 1228804
  612.5 1.0 copy-start.4
Sparse Core Ops, SparseCore 0:
  22.1 141.9 all-gather.4
  167.0 134.0 all-gather.6
  304.0 133.7 all-gather.8
  440.6 134.1 all-gather.10
  614.8 54.9 all-reduce.1
where the time goes:
time: 682 us; the launch traced here: 678 us
  waiting for transfers between devices  341 us (50%)
  blocking collectives  186 us (27%)
  matrix products  69.4 us (10%)
  local copies, waits for them, and re-layouts  48.2 us (7%)
  other arithmetic  17.4 us (3%)
  between operations  13.4 us (2%)
    all_gather x1, waiting for transfers between devices, per_device(): lax.all_gather(key_rows, 'seq', axis=0, tiled=True)  125 us
    all_gather x1, waiting for transfers between devices, per_device(): lax.all_gather(values, 'seq', axis=0, tiled=True)  97.4 us
    all_gather x1, blocking collectives, per_device(): lax.all_gather(row_delta.T, 'seq', axis=0, tiled=True)  80.1 us
    all_gather x1, blocking collectives, per_device(): lax.all_gather(log_total.T, 'seq', axis=0, tiled=True)  80 us
    all_gather x1, waiting for transfers between devices, per_device(): lax.all_gather(head_grads, 'seq', axis=0, tiled=True)  63.3 us
    psum x1, waiting for transfers between devices, per_device(): total_back = lax.psum(back_sum, 'tp')  55.1 us
    dynamic_slice x48, local copies, waits for them, and re-layouts, visit_block(): lax.dynamic_slice_in_dim(piece, first_row, block_size, 0)  47.7 us
    dot_general x16, matrix products, peak_step(): jnp.einsum('qhd,khd->hqk', query_heads, split_heads(key_part, heads_here)...  17.2 us
  transfers between devices with their start and end apart: 5, of which 4 were waited for; matrix products, arithmetic and copies ran while one was open for 14% of the time, Pallas kernels for 0%

commit v1 on v0

--- a/solution.py
+++ b/solution.py
@@ -210,7 +210,7 @@
     back_sum = back_sum + jnp.dot(key_done, w_key, preferred_element_type=jnp.float32)
     back_sum = back_sum + jnp.dot(value_done, w_value, preferred_element_type=jnp.float32)
     start_col = lax.axis_index("tp") * width_here
-    total_back = lax.psum(back_sum, "tp")
+    total_back = jnp.sum(lax.all_gather(back_sum, "tp"), axis=0)
     scaled = total_back * norm_gain[None, :]
     row_dot = jnp.sum(widened * scaled, axis=1, keepdims=True)
     branch = inverse * scaled - widened * inverse * inverse * inverse * row_dot / full_width

time: 682 us -> 667 us (0.978)
  the two profiles are of different devices: /device:TPU:8 before, /device:TPU:1 now
where the time goes in v1:
time: 667 us; the launch traced here: 664 us
  waiting for transfers between devices  360 us (54%)
  blocking collectives  152 us (23%)
  matrix products  69.1 us (10%)
  local copies, waits for them, and re-layouts  48.6 us (7%)
  other arithmetic  18.2 us (3%)
  between operations  13.4 us (2%)
    all_gather x1, waiting for transfers between devices, per_device(): lax.all_gather(key_rows, 'seq', axis=0, tiled=True)  122 us
    all_gather x1, waiting for transfers between devices, per_device(): lax.all_gather(values, 'seq', axis=0, tiled=True)  97.4 us
    all_gather x1, waiting for transfers between devices, per_device(): lax.all_gather(head_grads, 'seq', axis=0, tiled=True)  92.3 us
    all_gather x1, blocking collectives, per_device(): lax.all_gather(log_total.T, 'seq', axis=0, tiled=True)  65.6 us
    all_gather x1, blocking collectives, per_device(): lax.all_gather(row_delta.T, 'seq', axis=0, tiled=True)  65.5 us
    all_gather x1, waiting for transfers between devices, per_device(): total_back = jnp.sum(lax.all_gather(back_sum, 'tp'), axis=0)  48.3 us
    dynamic_slice x48, local copies, waits for them, and re-layouts, visit_block(): lax.dynamic_slice_in_dim(piece, first_row, block_size, 0)  47.7 us
    dot_general x16, matrix products, peak_step(): jnp.einsum('qhd,khd->hqk', query_heads, split_heads(key_part, heads_here)...  17.2 us
  transfers between devices with their start and end apart: 5, of which 4 were waited for; matrix products, arithmetic and copies ran while one was open for 14% of the time, Pallas kernels for 0%

profile of v1, /device:TPU:1, one launch (start us, length us, event | category | flops | bytes accessed | tf_op | source)
XLA Modules:
  0.0 664.2 jit_solution(12008940505054289163)
XLA Ops:
  6.6 11.0 %all_gather.31 = bf16[128,1280]{0,1:T(8,128)(2,1)S(1)} all-gather(bf16[128,320]{0,1:T(8,128)(2,1)} %param.15), channel_id=1, replica_groups=mesh['seq'=64,'tp'=4,'dp'=2] {'tp'}, dimensions={1}, use_global_device_ids=true | all-gather | bytes 409600 | tf_op jit(solution)/shard_map/all_gather | solution.py:55
  17.8 2.1 convolution_convert_fusion.2
  20.0 2.1 convolution_convert_fusion.1
  23.4 9.5 %all_gather.34 = bf16[128,1280]{0,1:T(8,128)(2,1)S(1)} all-gather(bf16[128,320]{0,1:T(8,128)(2,1)S(1)} %copy-done.6), channel_id=1, replica_groups=mesh['seq'=64,'tp'=4,'dp'=2] {'tp'}, dimensions={1}, use_global_device_ids=true | all-gather | bytes 409600 | tf_op jit(solution)/shard_map/all_gather | solution.py:56
  34.0 121.6 %all-gather.7.cloned.1.call-done = bf16[8192,160]{0,1:T(8,128)(2,1)} async-done(((bf16[128,160]{0,1:T(8,128)(2,1)}), bf16[8192,160]{0,1:T(8,128)(2,1)}) %all-gather.7.cloned.1.call-update) | async-done | bytes 2621456 | tf_op jit(solution)/shard_map/all_gather | solution.py:153
  155.6 39.6 %while.56 = (s32[]{:T(128)}, f32[2,128]{1,0:T(2,128)S(1)}, f32[2,128]{1,0:T(2,128)S(1)}, s32[64]{0:T(128)S(1)}, s32[128]{0:T(128)S(1)}, /*index=5*/bf16[8192,160...) while((s32[]{:T(128)}, f32[2,128]{1,0:T(2,128)S(1)}, ...), condition=%wide.region_6.7_spmd.clone, body=%wide.region_2.6_spmd.clone.sunk | while | flops 21806852 | bytes 1804210 | solution.py:43
  156.9 1.1 fusion.103
  159.3 1.1 fusion.103
  161.8 1.1 fusion.103
  164.3 1.1 fusion.103
  166.8 1.1 fusion.103
  169.2 1.1 fusion.103
  171.7 1.1 fusion.103
  174.2 1.1 fusion.103
  176.7 1.1 fusion.103
  179.1 1.1 fusion.103
  181.6 1.1 fusion.103
  184.1 1.1 fusion.103
  186.6 1.1 fusion.103
  189.0 1.1 fusion.103
  191.5 1.1 fusion.103
  194.0 1.1 fusion.103
  195.3 97.4 %all-gather.9.cloned.1.call-done = bf16[8192,160]{0,1:T(8,128)(2,1)} async-done(((bf16[128,160]{0,1:T(8,128)(2,1)}), bf16[8192,160]{0,1:T(8,128)(2,1)}) %all-gather.9.cloned.1.call-update) | async-done | bytes 2621456 | tf_op jit(solution)/shard_map/all_gather | solution.py:154
  292.6 50.2 %while.57 = (s32[]{:T(128)}, f32[2,128]{1,0:T(2,128)S(1)}, f32[2,128,80]{1,2,0:T(8,128)S(1)}, f32[2,128,80]{1,2,0:T(8,128)S(1)}, s32[64]{0:T(128)S(1)}, /*index=...) while((s32[]{:T(128)}, f32[2,128]{1,0:T(2,128)S(1)}, ...), condition=%wide.region_10.11_spmd.clone, body=%wide.region_7.10_spmd.clone.sunk | while | flops 84933376 | bytes 3966931 | solution.py:43
  293.9 1.1 fusion.115
  297.1 1.1 fusion.115
  300.2 1.1 fusion.115
  303.4 1.1 fusion.115
  306.5 1.1 fusion.115
  309.6 1.1 fusion.115
  312.8 1.1 fusion.115
  315.9 1.1 fusion.115
  319.1 1.1 fusion.115
  322.2 1.1 fusion.115
  325.3 1.1 fusion.115
  328.5 1.1 fusion.115
  331.6 1.1 fusion.115
  334.8 1.1 fusion.115
  337.9 1.1 fusion.115
  341.1 1.1 fusion.115
  342.9 65.5 %all_gather.38 = f32[8192,2]{0,1:T(2,128)S(1)} all-gather(f32[128,2]{0,1:T(2,128)S(1)} %bitcast.136), channel_id=1, replica_groups=mesh['seq'=64,'tp'=4,'dp'=2] {'seq'}, dimensions={0}, use_global_device_ids=true | all-gather | bytes 66560 | tf_op jit(solution)/shard_map/all_gather | solution.py:163
  408.4 65.6 %all_gather.36 = f32[8192,2]{0,1:T(2,128)S(1)} all-gather(f32[128,2]{0,1:T(2,128)S(1)} %bitcast.135), channel_id=1, replica_groups=mesh['seq'=64,'tp'=4,'dp'=2] {'seq'}, dimensions={0}, use_global_device_ids=true | all-gather | bytes 66560 | tf_op jit(solution)/shard_map/all_gather | solution.py:162
  474.0 92.3 %all-gather.13.cloned.1.call-done = bf16[8192,160]{0,1:T(8,128)(2,1)} async-done(((bf16[128,160]{0,1:T(8,128)(2,1)}), bf16[8192,160]{0,1:T(8,128)(2,1)}) %all-gather.13.cloned.1.call-update) | async-done | bytes 2621456 | tf_op jit(solution)/shard_map/all_gather | solution.py:203
  566.4 37.7 %while.58 = (s32[]{:T(128)}, f32[128,2,80]{0,2,1:T(8,128)S(1)}, f32[128,2,80]{0,2,1:T(8,128)S(1)}, bf16[8192,160]{0,1:T(8,128)(2,1)}, s32[128]{0:T(128)S(1)}, /*...) while((s32[]{:T(128)}, f32[128,2,80]{0,2,1:T(8,128)S(1)}, ...), condition=%wide.region_13.14_spmd.clone, body=%wide.region_11.13_spmd.clone.sunk | while | flops 84933120 | bytes 3462102 | solution.py:43
  566.4 1.1 constant_dynamic-slice_fusion.10
  605.0 1.1 convolution_add_fusion.2
  606.2 48.3 %all-gather.15.cloned.1.call-done = f32[512,1280]{1,0:T(8,128)} async-done(((f32[128,1280]{1,0:T(8,128)}), f32[512,1280]{1,0:T(8,128)}) %all-gather.15.cloned.1.call-update) | async-done | bytes 2621456 | tf_op jit(solution)/shard_map/all_gather | solution.py:213
  654.5 2.0 reduce_sum.118
  (491 shorter events, 93.6 us)
Async XLA Ops:
  6.5 15.7 %copy-start = (bf16[160,1280]{1,0:T(8,128)(2,1)S(1)}, bf16[160,1280]{1,0:T(8,128)(2,1)}, u32[]{:S(2)}) copy-start(bf16[160,1280]{1,0:T(8,128)(2,1)} %param.18) | copy-start | bytes 1228804
  6.5 15.7 %copy-start.9 = (f32[1280]{0:T(1024)S(1)}, f32[1280]{0:T(1024)}, u32[]{:S(2)}) copy-start(f32[1280]{0:T(1024)} %param.17) | copy-start | bytes 15364
  6.5 15.6 %copy-start.10 = (f32[80]{0:T(128)S(1)}, f32[80]{0:T(128)}, u32[]{:S(2)}) copy-start(f32[80]{0:T(128)} %param.22) | copy-start | bytes 964
  6.5 16.8 %copy-start.6 = (bf16[128,320]{0,1:T(8,128)(2,1)S(1)}, bf16[128,320]{0,1:T(8,128)(2,1)}, u32[]{:S(2)}) copy-start(bf16[128,320]{0,1:T(8,128)(2,1)} %param.16) | copy-start | bytes 245764
  6.5 26.3 %copy-start.5 = (bf16[160,1280]{1,0:T(8,128)(2,1)S(1)}, bf16[160,1280]{1,0:T(8,128)(2,1)}, u32[]{:S(2)}) copy-start(bf16[160,1280]{1,0:T(8,128)(2,1)} %param.21) | copy-start | bytes 1228804
  6.5 27.4 %copy-start.7 = (s32[64]{0:T(128)S(1)}, s32[64]{0:T(128)}, u32[]{:S(2)}) copy-start(s32[64]{0:T(128)} %param.23) | copy-start | bytes 772
  6.6 149.1 %all-gather.7.cloned.1.call-start = ((), (), s32[]{:S(2)}) async-start(), calls=%async_computation | async-start | bytes 2662400 | tf_op jit(solution)/shard_map/all_gather | solution.py:153
  19.9 272.7 %all-gather.9.cloned.1.call-start = ((), (), s32[]{:S(2)}) async-start(), calls=%async_computation.1 | async-start | bytes 2662400 | tf_op jit(solution)/shard_map/all_gather | solution.py:154
  22.0 452.0 %all-gather.11.cloned.1.call-start = ((), (), s32[]{:S(2)}) async-start(), calls=%async_computation.2 | async-start | bytes 2662400 | tf_op jit(solution)/shard_map/all_gather | solution.py:202
  23.3 543.1 %all-gather.13.cloned.1.call-start = ((), (), s32[]{:S(2)}) async-start(), calls=%async_computation.3 | async-start | bytes 2662400 | tf_op jit(solution)/shard_map/all_gather | solution.py:203
  33.8 620.7 %all-gather.15.cloned.1.call-start = ((), (), s32[]{:S(2)}) async-start(), calls=%async_computation.4 | async-start | bytes 3276800 | tf_op jit(solution)/shard_map/all_gather | solution.py:213
  155.6 137.0 %copy-start.1 = (bf16[128,160]{0,1:T(8,128)(2,1)S(1)}, bf16[128,160]{0,1:T(8,128)(2,1)}, u32[]{:S(2)}) copy-start(bf16[128,160]{0,1:T(8,128)(2,1)} %convolution_convert_fusion) | copy-start | bytes 122884
  292.6 273.7 %copy-start.2 = (bf16[128,160]{0,1:T(8,128)(2,1)S(1)}, bf16[128,160]{0,1:T(8,128)(2,1)}, u32[]{:S(2)}) copy-start(bf16[128,160]{0,1:T(8,128)(2,1)} %convolution_convert_fusion.1) | copy-start | bytes 122884
  292.6 273.7 %copy-start.8 = (bf16[128,160]{0,1:T(8,128)(2,1)S(1)}, bf16[128,160]{0,1:T(8,128)(2,1)}, u32[]{:S(2)}) copy-start(bf16[128,160]{0,1:T(8,128)(2,1)} %convolution_convert_fusion.2) | copy-start | bytes 122884
  566.4 38.1 %copy-start.3 = (bf16[160,1280]{1,0:T(8,128)(2,1)S(1)}, bf16[160,1280]{1,0:T(8,128)(2,1)}, u32[]{:S(2)}) copy-start(bf16[160,1280]{1,0:T(8,128)(2,1)} %param.19) | copy-start | bytes 1228804
  604.0 1.0 copy-start.4
Sparse Core Ops, SparseCore 0:
  20.0 135.5 all-gather.6
  158.6 134.0 all-gather.8
  295.6 134.9 all-gather.10
  433.3 132.9 all-gather.12
  606.3 48.1 all-gather.14
